TPU v7x, 256 devices: a whole 4x4x8 slice. The times are simulated.
256 devices in a mesh: ctx: 32 (over x, z), tp: 8 (over y, core).
Axes of the slice: x: 4, y: 4, z: 8, core: 2. Of those that a mesh axis runs over, the one named last changes fastest.
Arguments:
- query_in: bfloat16 [16384, 4096], P('ctx', 'tp'), may hold values from -6 to 6
- key_in: bfloat16 [16384, 4096], P('ctx', 'tp'), may hold values from -6 to 6
- value_in: bfloat16 [16384, 4096], P('ctx', 'tp'), may hold values from -6 to 6
- out_grad: bfloat16 [16384, 4096], P('ctx', 'tp'), may hold values from -6 to 6
- doc_ids: int32 [16384], replicated, may hold values from 0 to 15, never falling along the last dimension, each value on 1 to 2048 neighbouring positions
- skip_gain: float32 [4096], P('tp'), may hold values from -4 to 4
- filter_taps: bfloat16 [2048, 8], P(('ctx', 'tp')), may hold values from -0.125 to 0.125
Outputs:
- mixed_out: bfloat16 [16384, 4096], P('ctx', 'tp')
- query_grad: bfloat16 [16384, 4096], P('ctx', 'tp')
- key_grad: bfloat16 [16384, 4096], P('ctx', 'tp')
- value_grad: bfloat16 [16384, 4096], P('ctx', 'tp')
- filter_grad: float32 [2048, 8], P(('ctx', 'tp'))
Inputs may be any that keep to these rules, and one draw needn't show every extreme that they name: `doc_ids`: ids never fall along the tokens; each document is 1 to 2048 tokens long and one is exactly 2048 long.
All inputs are finite; a program needn't handle non-finite values.
Results may differ from a plain program's by a relative error of at most 0.0049.
Values may be sent and summed in bfloat16 or wider, within the bound.
No kernel may reach another device: no remote copies, remote signals or barrier semaphores. Data moves between devices by JAX's collectives and lax.ppermute only.
A program may use at most 128 MiB of HBM per device.

v0:
```python
import math
import jax
import jax.numpy as jnp
from jax import lax
from jax.sharding import PartitionSpec as P

MAXCH = 8
FGROUP = 512
FLEN = 2048


def shifted(value, axis, steps):
    count = lax.axis_size(axis)
    leading, last = (max(0, -steps), min(count, count - steps))
    return lax.ppermute(value, axis, [(source, source + steps) for source in range(leading, last)])


def band(window, rows, cols):
    groups_n = window.shape[0]
    flat = jnp.tile(window, (1, rows))[:, : rows * cols]
    return flat.reshape(groups_n, rows, cols)


def shards(query_in, key_in, value_in, out_grad, doc_ids, skip_gain, filter_taps):
    rows, width = query_in.shape
    groups_here = width // FGROUP
    here = lax.axis_index("ctx")
    span = -(-FLEN // rows)
    hist = span * rows
    wide = hist + rows
    assert hist == FLEN
    full_taps = lax.all_gather(filter_taps, ("ctx", "tp"), axis=0, tiled=True)
    first_group = lax.axis_index("tp") * groups_here
    taps = lax.dynamic_slice_in_dim(full_taps, first_group, groups_here, axis=1).T
    mixed_in = (key_in.astype(jnp.float32) * value_in.astype(jnp.float32)).astype(jnp.bfloat16)
    conv_grad = (out_grad.astype(jnp.float32) * query_in.astype(jnp.float32)).astype(jnp.bfloat16)
    ahead = [mixed_in]
    behind = [conv_grad]
    for _ in range(span):
        ahead.append(shifted(ahead[-1], "ctx", 1))
        behind.append(shifted(behind[-1], "ctx", -1))
    sources = jnp.concatenate(ahead[::-1], axis=0).reshape(wide, groups_here, FGROUP)
    readers = jnp.concatenate(behind, axis=0).reshape(wide, groups_here, FGROUP)
    ids_pad = jnp.concatenate(
        [jnp.full((hist,), -1, jnp.int32), doc_ids, jnp.full((hist,), -2, jnp.int32)]
    )
    ids_own = lax.dynamic_slice_in_dim(doc_ids, here * rows, rows)
    ids_src = lax.dynamic_slice_in_dim(ids_pad, here * rows, wide)
    ids_rdr = lax.dynamic_slice_in_dim(ids_pad, here * rows + hist, wide)
    same_src = ids_own[:, None] == ids_src[None, :]
    same_rdr = ids_own[:, None] == ids_rdr[None, :]
    zero_taps = jnp.zeros((groups_here, wide + 1 - FLEN), taps.dtype)
    fwd_window = jnp.concatenate([zero_taps[:, :1], taps[:, ::-1], zero_taps[:, 1:]], axis=1)
    bwd_window = jnp.concatenate([taps, zero_taps], axis=1)
    fwd_tile = jnp.where(same_src[None], band(fwd_window, rows, wide), 0)
    bwd_tile = jnp.where(same_rdr[None], band(bwd_window, rows, wide), 0)
    skip = skip_gain.reshape(groups_here, FGROUP)
    own_src = mixed_in.reshape(rows, groups_here, FGROUP)
    own_grad = conv_grad.reshape(rows, groups_here, FGROUP)
    conv = skip * own_src.astype(jnp.float32) + jnp.einsum(
        "gab,bgc->agc", fwd_tile, sources, preferred_element_type=jnp.float32
    )
    mixed_grad = skip * own_grad.astype(jnp.float32) + jnp.einsum(
        "gab,bgc->agc", bwd_tile, readers, preferred_element_type=jnp.float32
    )
    product = jnp.einsum("agc,bgc->gab", own_grad, sources, preferred_element_type=jnp.float32)
    product = jnp.where(same_src[None], product, 0.0)
    skewed = jnp.pad(product.reshape(groups_here, rows * wide), ((0, 0), (0, rows)))
    diag = jnp.sum(skewed.reshape(groups_here, rows, wide + 1), axis=1)
    filter_part = diag[:, 1 : hist + 1][:, ::-1]
    conv = conv.reshape(rows, width)
    mixed_grad = mixed_grad.reshape(rows, width)
    mixed_out = (query_in.astype(jnp.float32) * conv).astype(jnp.bfloat16)
    query_grad = (out_grad.astype(jnp.float32) * conv).astype(jnp.bfloat16)
    key_grad = (mixed_grad * value_in.astype(jnp.float32)).astype(jnp.bfloat16)
    value_grad = (mixed_grad * key_in.astype(jnp.float32)).astype(jnp.bfloat16)
    placed = jnp.zeros((FLEN, full_taps.shape[1]), jnp.float32)
    placed = lax.dynamic_update_slice_in_dim(placed, filter_part.T, first_group, axis=1)
    summed = lax.psum_scatter(placed, ("ctx", "tp"), scatter_dimension=0, tiled=True)
    tokens = lax.axis_size("ctx") * rows
    filter_grad = summed * (1.0 / math.sqrt(FGROUP * tokens))
    return (mixed_out, query_grad, key_grad, value_grad, filter_grad)


def solution(mesh):
    in_specs = (
        P("ctx", "tp"),
        P("ctx", "tp"),
        P("ctx", "tp"),
        P("ctx", "tp"),
        P(),
        P("tp"),
        P(("ctx", "tp"), None),
    )
    out_specs = (
        P("ctx", "tp"),
        P("ctx", "tp"),
        P("ctx", "tp"),
        P("ctx", "tp"),
        P(("ctx", "tp"), None),
    )
    return jax.shard_map(shards, mesh=mesh, in_specs=in_specs, out_specs=out_specs, check_vma=False)
```

profile of v0, /device:TPU:2, one launch (start us, length us, event | category | flops | bytes accessed | tf_op | source)
XLA Modules:
  0.0 723.5 jit_solution(13073037169013701247)
XLA Ops:
  10.9 7.7 %collective-permute-start.4 = (bf16[512,512]{0,1:T(8,128)(2,1)S(1)}, bf16[512,512]{0,1:T(8,128)(2,1)S(1)}, u32[]{:S(2)}, u32[]{:S(2)}) collective-permute-start(bf16[512,512]{0,1:T(8,128)(2,1)S(1)} %get-tuple-element.23), channel_id=1, source_target_pairs={{8,0},{16,8},{24,16},{32,24},{40,32},{48,40},{56,48},{64,56},{72,6... | collective-permute-start | bytes 1572872 | tf_op jit(solution)/shard_map/ppermute | solution.py:15
  18.8 11.0 %collective-permute-done.4 = bf16[512,512]{0,1:T(8,128)(2,1)S(1)} collective-permute-done((bf16[512,512]{0,1:T(8,128)(2,1)S(1)}, bf16[512,512]{0,1:T(8,128)(2,1)S(1)}, u32[]{:S(2)}, u32[]{:S(2)}) %collective-permute-start.4) | collective-permute-done | bytes 524320 | tf_op jit(solution)/shard_map/ppermute | solution.py:15
  29.8 6.5 collective-permute-start.5
  36.3 5.3 broadcast_bitcast_fusion
  41.6 10.2 %copy.39 = s32[1,1,512,2560]{3,1,2,0:T(1,128)} copy(s32[1,1,512,2560]{3,2,1,0:T(8,128)} %get-tuple-element.32) | data formatting | bytes 10485760
  51.8 10.5 %copy.40 = s32[1,1,512,2560]{3,1,2,0:T(1,128)} copy(s32[1,1,512,2560]{3,2,1,0:T(8,128)} %get-tuple-element.31) | data formatting | bytes 10485760
  64.2 2.7 broadcast_bitcast_fusion.2
  67.0 10.2 %copy.38 = s32[1,1,512,2560]{3,1,2,0:T(1,128)} copy(s32[1,1,512,2560]{3,2,1,0:T(8,128)} %broadcast_bitcast_fusion.2) | data formatting | bytes 10485760
  77.1 67.7 %all_gather.3 = bf16[2048,8]{1,0:T(8,128)(2,1)S(1)} all-gather(bf16[8,8]{1,0:T(8,128)(2,1)S(1)} %copy-done.17), channel_id=1, replica_groups=mesh['ctx'=32,'tp'=8] {'ctx','tp'}, dimensions={0}, use_global_device_ids=true | all-gather | bytes 32896 | tf_op jit(solution)/shard_map/all_gather | solution.py:32
  147.5 5.8 reshape.151
  153.3 26.5 %tile.24 = bf16[1,1311232]{1,0:T(2,128)(2,1)} reshape(bf16[1311232]{0:T(1024)(128)(2,1)} %reshape.151) | data formatting | bytes 5244928 | tf_op jit(solution)/shard_map/tile | solution.py:20
  180.0 5.8 reshape.153
  185.8 26.6 %tile.27 = bf16[1,1311232]{1,0:T(2,128)(2,1)} reshape(bf16[1311232]{0:T(1024)(128)(2,1)} %reshape.153) | data formatting | bytes 5244928 | tf_op jit(solution)/shard_map/tile | solution.py:20
  212.5 4.6 collective-permute-start.7
  217.1 58.1 %fusion.1 = (bf16[1310720]{0:T(1024)(128)(2,1)}, bf16[1310720]{0:T(1024)(128)(2,1)S(1)}) fusion(bf16[1,1311232]{1,0:T(2,128)(2,1)} %tile.27, s32[1,1310720]{1,0:T(1,128)} %bitcast.50, s32[1,1310720]{1,0:T(1,128)} %bitcast.49, bf16[1,1311232]{1,0:T(2,128)(2,1)} %tile.24, s32[1,1310720]{1,0:T(1,128)} %bitcast.48), kind=kLoop, calls=%fused_computation.5 | loop fusion | flops 5242880 | bytes 26214400 | tf_op jit(solution)/shard_map/jit(_where)/select_n | solution.py:56
  275.2 6.1 select_n.44
  293.3 4.4 fusion.7
  300.4 16.0 %collective-permute-done = bf16[512,512]{0,1:T(8,128)(2,1)S(1)} collective-permute-done((bf16[512,512]{0,1:T(8,128)(2,1)S(1)}, bf16[512,512]{0,1:T(8,128)(2,1)S(1)}, u32[]{:S(2)}, u32[]{:S(2)}) %collective-permute-start) | collective-permute-done | bytes 524320 | tf_op jit(solution)/shard_map/ppermute | solution.py:15
  319.1 15.1 %collective-permute-done.1 = bf16[512,512]{0,1:T(8,128)(2,1)S(1)} collective-permute-done((bf16[512,512]{0,1:T(8,128)(2,1)S(1)}, bf16[512,512]{0,1:T(8,128)(2,1)S(1)}, u32[]{:S(2)}, u32[]{:S(2)}) %collective-permute-start.1) | collective-permute-done | bytes 524320 | tf_op jit(solution)/shard_map/ppermute | solution.py:15
  337.0 14.4 %collective-permute-done.2 = bf16[512,512]{0,1:T(8,128)(2,1)} collective-permute-done((bf16[512,512]{0,1:T(8,128)(2,1)S(1)}, bf16[512,512]{0,1:T(8,128)(2,1)}, u32[]{:S(2)}, u32[]{:S(2)}) %collective-permute-start.2) | collective-permute-done | bytes 524320 | tf_op jit(solution)/shard_map/ppermute | solution.py:15
  353.3 4.1 select_n.41
  357.4 2.1 copy.36
  359.6 2.1 copy.37
  361.7 5.3 collective-permute-done.3
  370.8 3.9 select_bitcast_fusion
  374.8 10.1 %copy.41 = f32[1,1,512,2560]{3,1,2,0:T(1,128)} copy(f32[1,1,512,2560]{3,2,1,0:T(8,128)} %select_bitcast_fusion) | data formatting | bytes 10485760
  384.9 57.9 %pad_reduce_fusion = f32[1311232]{0:T(1024)} fusion(f32[1,1310720]{1,0:T(1,128)} %bitcast.47), kind=kLoop, calls=%fused_computation.2 | loop fusion | bytes 10487808 | tf_op jit(solution)/shard_map/jit(_pad)/pad | solution.py:68
  442.8 8.6 %reshape.144 = f32[512,2561]{1,0:T(8,128)} reshape(f32[1311232]{0:T(1024)} %pad_reduce_fusion) | data formatting | bytes 10489856 | tf_op jit(solution)/shard_map/reshape | solution.py:69
  451.4 2.8 reduce_sum.11
  456.2 3.9 dynamic_update_slice.3
  461.2 4.3 fusion.10
  467.5 247.4 %all-reduce.5.cloned.1.call-done = f32[2048,8]{1,0:T(8,128)} async-done(((f32[2048,8]{1,0:T(8,128)}), f32[2048,8]{1,0:T(8,128)}) %all-reduce.5.cloned.1.call-update) | async-done | bytes 65552
  (84 shorter events, 40.7 us)
Async XLA Ops:
  7.2 11.5 %copy-start.16 = (s32[16384]{0:T(1024)S(1)}, s32[16384]{0:T(1024)}, u32[]{:S(2)}) copy-start(s32[16384]{0:T(1024)} %param.11) | copy-start | bytes 196612
  7.2 707.7 %all-reduce.5.cloned.1.call-start = ((), (), s32[]{:S(2)}) async-start(), calls=%async_computation | async-start | bytes 2097152
  8.5 33.1 %copy-start.3 = (bf16[512,512]{0,1:T(8,128)(2,1)}, bf16[512,512]{0,1:T(8,128)(2,1)S(1)}, u32[]{:S(2)}) copy-start(bf16[512,512]{0,1:T(8,128)(2,1)S(1)} %copy.29) | copy-start | bytes 1572868
  9.9 31.7 %copy-start.5 = (bf16[512,512]{0,1:T(8,128)(2,1)}, bf16[512,512]{0,1:T(8,128)(2,1)S(1)}, u32[]{:S(2)}) copy-start(bf16[512,512]{0,1:T(8,128)(2,1)S(1)} %copy.32) | copy-start | bytes 1572868
  10.9 18.9 %collective-permute-start.4 = (bf16[512,512]{0,1:T(8,128)(2,1)S(1)}, bf16[512,512]{0,1:T(8,128)(2,1)S(1)}, u32[]{:S(2)}, u32[]{:S(2)}) collective-permute-start(bf16[512,512]{0,1:T(8,128)(2,1)S(1)} %get-tuple-element.23), channel_id=1, source_target_pairs={{8,0},{16,8},{24,16},{32,24},{40,32},{48,40},{56,48},{64,56},{72,6... | collective-permute-start | bytes 1572872 | tf_op jit(solution)/shard_map/ppermute | solution.py:15
  29.8 11.8 %copy-start.7 = (bf16[512,512]{0,1:T(8,128)(2,1)}, bf16[512,512]{0,1:T(8,128)(2,1)S(1)}, u32[]{:S(2)}) copy-start(bf16[512,512]{0,1:T(8,128)(2,1)S(1)} %collective-permute-done.4) | copy-start | bytes 1572868
  29.8 32.5 %collective-permute-start.5 = (bf16[512,512]{0,1:T(8,128)(2,1)S(1)}, bf16[512,512]{0,1:T(8,128)(2,1)}, u32[]{:S(2)}, u32[]{:S(2)}) collective-permute-start(bf16[512,512]{0,1:T(8,128)(2,1)S(1)} %collective-permute-done.4), channel_id=1, source_target_pairs={{8,0},{16,8},{24,16},{32,24},{40,32},{48,40},{56,48},{64,56},{72,6... | collective-permute-start | bytes 1572872 | tf_op jit(solution)/shard_map/ppermute | solution.py:15
  62.3 150.2 %collective-permute-start.6 = (bf16[512,512]{0,1:T(8,128)(2,1)}, bf16[512,512]{0,1:T(8,128)(2,1)}, u32[]{:S(2)}, u32[]{:S(2)}) collective-permute-start(bf16[512,512]{0,1:T(8,128)(2,1)} %collective-permute-done.5), channel_id=1, source_target_pairs={{8,0},{16,8},{24,16},{32,24},{40,32},{48,40},{56,48},{64,56},{72,6... | collective-permute-start | bytes 1572872 | tf_op jit(solution)/shard_map/ppermute | solution.py:15
  67.0 10.2 %copy-start.17 = (bf16[8,8]{1,0:T(8,128)(2,1)S(1)}, bf16[8,8]{1,0:T(8,128)(2,1)}, u32[]{:S(2)}) copy-start(bf16[8,8]{1,0:T(8,128)(2,1)} %param.13) | copy-start | bytes 388
  212.5 78.9 %collective-permute-start.7 = (bf16[512,512]{0,1:T(8,128)(2,1)}, bf16[512,512]{0,1:T(8,128)(2,1)}, u32[]{:S(2)}, u32[]{:S(2)}) collective-permute-start(bf16[512,512]{0,1:T(8,128)(2,1)} %collective-permute-done.6), channel_id=1, source_target_pairs={{8,0},{16,8},{24,16},{32,24},{40,32},{48,40},{56,48},{64,56},{72,6... | collective-permute-start | bytes 1572872 | tf_op jit(solution)/shard_map/ppermute | solution.py:15
  283.3 9.9 %copy-start.18 = (f32[512]{0:T(512)S(1)}, f32[512]{0:T(512)}, u32[]{:S(2)}) copy-start(f32[512]{0:T(512)} %param.12) | copy-start | bytes 6148
  285.4 7.9 %copy-start.2 = (bf16[512,2560]{1,0:T(8,128)(2,1)S(1)}, bf16[512,2560]{1,0:T(8,128)(2,1)}, u32[]{:S(2)}) copy-start(bf16[512,2560]{1,0:T(8,128)(2,1)} %select_n.44) | copy-start | bytes 7864324
  285.4 7.9 %copy-start.14 = (bf16[512,512]{0,1:T(8,128)(2,1)S(1)}, bf16[512,512]{0,1:T(8,128)(2,1)}, u32[]{:S(2)}) copy-start(bf16[512,512]{0,1:T(8,128)(2,1)} %copy.30) | copy-start | bytes 1572868
  285.4 7.9 %copy-start.15 = (bf16[512,512]{0,1:T(8,128)(2,1)S(1)}, bf16[512,512]{0,1:T(8,128)(2,1)}, u32[]{:S(2)}) copy-start(bf16[512,512]{0,1:T(8,128)(2,1)} %copy.31) | copy-start | bytes 1572868
  297.7 0.8 copy-start.8
  298.5 17.9 %collective-permute-start = (bf16[512,512]{0,1:T(8,128)(2,1)S(1)}, bf16[512,512]{0,1:T(8,128)(2,1)S(1)}, u32[]{:S(2)}, u32[]{:S(2)}) collective-permute-start(bf16[512,512]{0,1:T(8,128)(2,1)S(1)} %get-tuple-element.26), channel_id=1, source_target_pairs={{0,8},{8,16},{16,24},{24,32},{32,40},{40,48},{48,56},{56,64},{64,7... | collective-permute-start | bytes 1572872 | tf_op jit(solution)/shard_map/ppermute | solution.py:15
  316.4 0.8 copy-start.10
  317.2 17.0 %collective-permute-start.1 = (bf16[512,512]{0,1:T(8,128)(2,1)S(1)}, bf16[512,512]{0,1:T(8,128)(2,1)S(1)}, u32[]{:S(2)}, u32[]{:S(2)}) collective-permute-start(bf16[512,512]{0,1:T(8,128)(2,1)S(1)} %collective-permute-done), channel_id=1, source_target_pairs={{0,8},{8,16},{16,24},{24,32},{32,40},{40,48},{48,56},{56,64},{64,7... | collective-permute-start | bytes 1572872 | tf_op jit(solution)/shard_map/ppermute | solution.py:15
  334.3 0.8 copy-start.12
  335.1 16.3 %collective-permute-start.2 = (bf16[512,512]{0,1:T(8,128)(2,1)S(1)}, bf16[512,512]{0,1:T(8,128)(2,1)}, u32[]{:S(2)}, u32[]{:S(2)}) collective-permute-start(bf16[512,512]{0,1:T(8,128)(2,1)S(1)} %collective-permute-done.1), channel_id=1, source_target_pairs={{0,8},{8,16},{16,24},{24,32},{32,40},{40,48},{48,56},{56,64},{64,7... | collective-permute-start | bytes 1572872 | tf_op jit(solution)/shard_map/ppermute | solution.py:15
  351.4 15.6 %collective-permute-start.3 = (bf16[512,512]{0,1:T(8,128)(2,1)}, bf16[512,512]{0,1:T(8,128)(2,1)}, u32[]{:S(2)}, u32[]{:S(2)}) collective-permute-start(bf16[512,512]{0,1:T(8,128)(2,1)} %collective-permute-done.2), channel_id=1, source_target_pairs={{0,8},{8,16},{16,24},{24,32},{32,40},{40,48},{48,56},{56,64},{64,7... | collective-permute-start | bytes 1572872 | tf_op jit(solution)/shard_map/ppermute | solution.py:15
  357.4 11.8 %copy-start.13 = (bf16[512,512]{0,1:T(8,128)(2,1)S(1)}, bf16[512,512]{0,1:T(8,128)(2,1)}, u32[]{:S(2)}) copy-start(bf16[512,512]{0,1:T(8,128)(2,1)} %copy-done.12) | copy-start | bytes 1572868
  357.4 11.8 %copy-start.11 = (bf16[512,512]{0,1:T(8,128)(2,1)S(1)}, bf16[512,512]{0,1:T(8,128)(2,1)}, u32[]{:S(2)}) copy-start(bf16[512,512]{0,1:T(8,128)(2,1)} %copy-done.10) | copy-start | bytes 1572868
  359.6 9.7 %copy-start.9 = (bf16[512,512]{0,1:T(8,128)(2,1)S(1)}, bf16[512,512]{0,1:T(8,128)(2,1)}, u32[]{:S(2)}) copy-start(bf16[512,512]{0,1:T(8,128)(2,1)} %copy-done.8) | copy-start | bytes 1572868
  369.3 1.5 copy-start.1
  455.8 5.4 copy-start.4
  455.8 5.4 copy-start.6
  460.2 1.0 copy-start
Sparse Core Ops, SparseCore 0:
  461.3 253.5 all-reduce.4
where the time goes:
time: 734 us; the launch traced here: 723 us
  waiting for transfers between devices  309 us (42%)
  local copies, waits for them, and re-layouts  227 us (31%)
  blocking collectives  67.7 us (9%)
  other arithmetic  63.3 us (9%)
  starting transfers between devices  28.4 us (4%)
  between operations  14.8 us (2%)
  matrix products  12.6 us (2%)
    unnamed x2, waiting for transfers between devices  247 us
    unnamed x61, local copies, waits for them, and re-layouts  86.8 us
    all_gather x1, blocking collectives, shards(): full_taps = lax.all_gather(filter_taps, ('ctx', 'tp'), axis=0, tiled=True)  67.7 us
    ppermute x8, waiting for transfers between devices, shifted(): lax.ppermute(value, axis, [(source, source + steps) for source in range(l...  61.9 us
    select_n x1, other arithmetic, shards(): bwd_tile = jnp.where(same_rdr[None], band(bwd_window, rows, wide), 0)  58.1 us
    pad x1, local copies, waits for them, and re-layouts, shards(): jnp.pad(product.reshape(groups_here, rows * wide), ((0, 0), (0, rows)))  57.9 us
    another operation x4, local copies, waits for them, and re-layouts, band(): flat = jnp.tile(window, (1, rows))[:, :rows * cols]  53.5 us
    ppermute x8, starting transfers between devices, shifted(): lax.ppermute(value, axis, [(source, source + steps) for source in range(l...  28.4 us
  transfers between devices with their start and end apart: 9, of which 6 were waited for; matrix products, arithmetic and copies ran while one was open for 27% of the time, Pallas kernels for 0%

commit v1 on v0

--- a/solution.py
+++ b/solution.py
@@ -29,7 +29,12 @@
     hist = span * rows
     wide = hist + rows
     assert hist == FLEN
-    full_taps = lax.all_gather(filter_taps, ("ctx", "tp"), axis=0, tiled=True)
+    full_taps = jnp.concatenate(
+        lax.all_to_all(
+            jnp.stack([filter_taps] * lax.axis_size(("ctx", "tp"))), ("ctx", "tp"), 0, 0
+        ),
+        axis=0,
+    )
     first_group = lax.axis_index("tp") * groups_here
     taps = lax.dynamic_slice_in_dim(full_taps, first_group, groups_here, axis=1).T
     mixed_in = (key_in.astype(jnp.float32) * value_in.astype(jnp.float32)).astype(jnp.bfloat16)

time: 734 us -> 670 us (0.913)
  blocking collectives: 67.7 us -> 0 us
  starting transfers between devices: 28.4 us -> 42.8 us
    all_gather x1 -> x0, blocking collectives: 67.7 us -> none  [shards(): full_taps = lax.all_gather(filter_taps, ('ctx', 'tp'), axis=0, tiled=True)]
    all_to_all x0 -> x1, starting transfers between devices: none -> 9.42 us  [shards(): lax.all_to_all(jnp.stack([filter_taps] * lax.axis_size(('ctx', 'tp'))), (...]
    ppermute x8, waiting for transfers between devices: 61.9 us -> 53.7 us  [shifted(): lax.ppermute(value, axis, [(source, source + steps) for source in range(l...]
    unnamed x61 -> x66, local copies, waits for them, and re-layouts: 86.8 us -> 85 us
  transfers between devices with their start and end apart: 9 -> 10, of which waited for: 6 -> 7; matrix products, arithmetic and copies ran while one was open for 27% -> 29% of each run, Pallas kernels for 0% -> 0%
where the time goes in v1:
time: 670 us; the launch traced here: 666 us
  waiting for transfers between devices  306 us (46%)
  local copies, waits for them, and re-layouts  226 us (34%)
  other arithmetic  63.3 us (9%)
  starting transfers between devices  42.8 us (6%)
  between operations  14.6 us (2%)
  matrix products  12.6 us (2%)
    unnamed x2, waiting for transfers between devices  252 us
    unnamed x66, local copies, waits for them, and re-layouts  85 us
    select_n x1, other arithmetic, shards(): bwd_tile = jnp.where(same_rdr[None], band(bwd_window, rows, wide), 0)  58.1 us
    pad x1, local copies, waits for them, and re-layouts, shards(): jnp.pad(product.reshape(groups_here, rows * wide), ((0, 0), (0, rows)))  57.9 us
    ppermute x8, waiting for transfers between devices, shifted(): lax.ppermute(value, axis, [(source, source + steps) for source in range(l...  53.7 us
    another operation x4, local copies, waits for them, and re-layouts, band(): flat = jnp.tile(window, (1, rows))[:, :rows * cols]  53.5 us
    ppermute x8, starting transfers between devices, shifted(): lax.ppermute(value, axis, [(source, source + steps) for source in range(l...  33.3 us
  transfers between devices with their start and end apart: 10, of which 7 were waited for; matrix products, arithmetic and copies ran while one was open for 29% of the time, Pallas kernels for 0%

profile of v1, /device:TPU:2, one launch (start us, length us, event | category | flops | bytes accessed | tf_op | source)
XLA Modules:
  0.0 665.9 jit_solution(17988695364169417431)
XLA Ops:
  10.9 7.7 %collective-permute-start.4 = (bf16[512,512]{0,1:T(8,128)(2,1)S(1)}, bf16[512,512]{0,1:T(8,128)(2,1)S(1)}, u32[]{:S(2)}, u32[]{:S(2)}) collective-permute-start(bf16[512,512]{0,1:T(8,128)(2,1)S(1)} %get-tuple-element.28), channel_id=1, source_target_pairs={{8,0},{16,8},{24,16},{32,24},{40,32},{48,40},{56,48},{64,56},{72,6... | collective-permute-start | bytes 1572872 | tf_op jit(solution)/shard_map/ppermute | solution.py:15
  19.6 9.4 %all-to-all-start = ((bf16[256,8,8]{1,2,0:T(8,128)(2,1)}), bf16[256,8,8]{1,2,0:T(8,128)(2,1)S(1)}, u32[]{:S(2)}, u32[]{:S(2)}) async-start(bf16[256,8,8]{1,2,0:T(8,128)(2,1)} %stack.2), calls=%async_computation | async-start | bytes 1048576 | tf_op jit(solution)/shard_map/all_to_all | solution.py:33
  29.3 4.0 collective-permute-done.4
  33.3 7.5 %collective-permute-start.5 = (bf16[512,512]{0,1:T(8,128)(2,1)S(1)}, bf16[512,512]{0,1:T(8,128)(2,1)}, u32[]{:S(2)}, u32[]{:S(2)}) collective-permute-start(bf16[512,512]{0,1:T(8,128)(2,1)S(1)} %collective-permute-done.4), channel_id=1, source_target_pairs={{8,0},{16,8},{24,16},{32,24},{40,32},{48,40},{56,48},{64,56},{72,6... | collective-permute-start | bytes 1572872 | tf_op jit(solution)/shard_map/ppermute | solution.py:15
  40.8 5.2 broadcast_bitcast_fusion
  46.0 6.5 collective-permute-done.5
  52.5 6.6 collective-permute-start.6
  59.1 2.7 broadcast_bitcast_fusion.2
  61.8 10.2 %copy.52 = s32[1,1,512,2560]{3,1,2,0:T(1,128)} copy(s32[1,1,512,2560]{3,2,1,0:T(8,128)} %get-tuple-element.37) | data formatting | bytes 10485760
  72.0 10.3 %copy.53 = s32[1,1,512,2560]{3,1,2,0:T(1,128)} copy(s32[1,1,512,2560]{3,2,1,0:T(8,128)} %get-tuple-element.36) | data formatting | bytes 10485760
  82.3 10.6 %copy.51 = s32[1,1,512,2560]{3,1,2,0:T(1,128)} copy(s32[1,1,512,2560]{3,2,1,0:T(8,128)} %broadcast_bitcast_fusion.2) | data formatting | bytes 10485760
  97.5 5.8 reshape.156
  103.4 26.5 %tile.24 = bf16[1,1311232]{1,0:T(2,128)(2,1)} reshape(bf16[1311232]{0:T(1024)(128)(2,1)} %reshape.156) | data formatting | bytes 5244928 | tf_op jit(solution)/shard_map/tile | solution.py:20
  130.1 5.8 reshape.158
  135.9 26.6 %tile.27 = bf16[1,1311232]{1,0:T(2,128)(2,1)} reshape(bf16[1311232]{0:T(1024)(128)(2,1)} %reshape.158) | data formatting | bytes 5244928 | tf_op jit(solution)/shard_map/tile | solution.py:20
  164.5 58.1 %fusion.1 = (bf16[1310720]{0:T(1024)(128)(2,1)}, bf16[1310720]{0:T(1024)(128)(2,1)S(1)}) fusion(bf16[1,1311232]{1,0:T(2,128)(2,1)} %tile.27, s32[1,1310720]{1,0:T(1,128)} %bitcast.54, s32[1,1310720]{1,0:T(1,128)} %bitcast.53, bf16[1,1311232]{1,0:T(2,128)(2,1)} %tile.24, s32[1,1310720]{1,0:T(1,128)} %bitcast.52), kind=kLoop, calls=%fused_computation.5 | loop fusion | flops 5242880 | bytes 26214400 | tf_op jit(solution)/shard_map/jit(_where)/select_n | solution.py:61
  222.6 6.1 select_n.44
  236.6 4.4 fusion.7
  241.8 3.9 collective-permute-start
  245.7 12.6 %collective-permute-done = bf16[512,512]{0,1:T(8,128)(2,1)S(1)} collective-permute-done((bf16[512,512]{0,1:T(8,128)(2,1)S(1)}, bf16[512,512]{0,1:T(8,128)(2,1)S(1)}, u32[]{:S(2)}, u32[]{:S(2)}) %collective-permute-start) | collective-permute-done | bytes 524320 | tf_op jit(solution)/shard_map/ppermute | solution.py:15
  261.0 13.7 %collective-permute-done.1 = bf16[512,512]{0,1:T(8,128)(2,1)S(1)} collective-permute-done((bf16[512,512]{0,1:T(8,128)(2,1)S(1)}, bf16[512,512]{0,1:T(8,128)(2,1)S(1)}, u32[]{:S(2)}, u32[]{:S(2)}) %collective-permute-start.1) | collective-permute-done | bytes 524320 | tf_op jit(solution)/shard_map/ppermute | solution.py:15
  277.4 13.0 %collective-permute-done.2 = bf16[512,512]{0,1:T(8,128)(2,1)} collective-permute-done((bf16[512,512]{0,1:T(8,128)(2,1)S(1)}, bf16[512,512]{0,1:T(8,128)(2,1)}, u32[]{:S(2)}, u32[]{:S(2)}) %collective-permute-start.2) | collective-permute-done | bytes 524320 | tf_op jit(solution)/shard_map/ppermute | solution.py:15
  292.3 4.1 select_n.41
  300.7 4.0 collective-permute-done.3
  308.5 3.9 select_bitcast_fusion
  312.4 10.2 %copy.54 = f32[1,1,512,2560]{3,1,2,0:T(1,128)} copy(f32[1,1,512,2560]{3,2,1,0:T(8,128)} %select_bitcast_fusion) | data formatting | bytes 10485760
  322.6 57.9 %pad_reduce_fusion = f32[1311232]{0:T(1024)} fusion(f32[1,1310720]{1,0:T(1,128)} %bitcast.51), kind=kLoop, calls=%fused_computation.2 | loop fusion | bytes 10487808 | tf_op jit(solution)/shard_map/jit(_pad)/pad | solution.py:73
  380.5 8.6 %reshape.150 = f32[512,2561]{1,0:T(8,128)} reshape(f32[1311232]{0:T(1024)} %pad_reduce_fusion) | data formatting | bytes 10489856 | tf_op jit(solution)/shard_map/reshape | solution.py:74
  389.1 2.8 reduce_sum.11
  393.9 3.9 dynamic_update_slice.3
  398.9 4.3 fusion.10
  405.2 252.4 %all-reduce.5.cloned.1.call-done = f32[2048,8]{1,0:T(8,128)} async-done(((f32[2048,8]{1,0:T(8,128)}), f32[2048,8]{1,0:T(8,128)}) %all-reduce.5.cloned.1.call-update) | async-done | bytes 65552
  (92 shorter events, 41.8 us)
Async XLA Ops:
  7.2 11.5 %copy-start.19 = (bf16[8,8]{1,0:T(8,128)(2,1)S(1)}, bf16[8,8]{1,0:T(8,128)(2,1)}, u32[]{:S(2)}) copy-start(bf16[8,8]{1,0:T(8,128)(2,1)} %param.13) | copy-start | bytes 388
  8.4 11.2 %copy-start.3 = (bf16[512,512]{0,1:T(8,128)(2,1)}, bf16[512,512]{0,1:T(8,128)(2,1)S(1)}, u32[]{:S(2)}) copy-start(bf16[512,512]{0,1:T(8,128)(2,1)S(1)} %copy.40) | copy-start | bytes 1572868
  8.4 20.6 %copy-start.18 = (s32[16384]{0:T(1024)S(1)}, s32[16384]{0:T(1024)}, u32[]{:S(2)}) copy-start(s32[16384]{0:T(1024)} %param.11) | copy-start | bytes 196612
  9.9 36.1 %copy-start.5 = (bf16[512,512]{0,1:T(8,128)(2,1)}, bf16[512,512]{0,1:T(8,128)(2,1)S(1)}, u32[]{:S(2)}) copy-start(bf16[512,512]{0,1:T(8,128)(2,1)S(1)} %copy.45) | copy-start | bytes 1572868
  10.9 22.4 %collective-permute-start.4 = (bf16[512,512]{0,1:T(8,128)(2,1)S(1)}, bf16[512,512]{0,1:T(8,128)(2,1)S(1)}, u32[]{:S(2)}, u32[]{:S(2)}) collective-permute-start(bf16[512,512]{0,1:T(8,128)(2,1)S(1)} %get-tuple-element.28), channel_id=1, source_target_pairs={{8,0},{16,8},{24,16},{32,24},{40,32},{48,40},{56,48},{64,56},{72,6... | collective-permute-start | bytes 1572872 | tf_op jit(solution)/shard_map/ppermute | solution.py:15
  19.6 75.3 %all-to-all-start = ((bf16[256,8,8]{1,2,0:T(8,128)(2,1)}), bf16[256,8,8]{1,2,0:T(8,128)(2,1)S(1)}, u32[]{:S(2)}, u32[]{:S(2)}) async-start(bf16[256,8,8]{1,2,0:T(8,128)(2,1)} %stack.2), calls=%async_computation | async-start | bytes 1048576 | tf_op jit(solution)/shard_map/all_to_all | solution.py:33
  29.0 628.5 %all-reduce.5.cloned.1.call-start = ((), (), s32[]{:S(2)}) async-start(), calls=%async_computation.1 | async-start | bytes 2097152
  33.3 12.8 %copy-start.9 = (bf16[512,512]{0,1:T(8,128)(2,1)}, bf16[512,512]{0,1:T(8,128)(2,1)S(1)}, u32[]{:S(2)}) copy-start(bf16[512,512]{0,1:T(8,128)(2,1)S(1)} %collective-permute-done.4) | copy-start | bytes 1572868
  33.3 19.2 %collective-permute-start.5 = (bf16[512,512]{0,1:T(8,128)(2,1)S(1)}, bf16[512,512]{0,1:T(8,128)(2,1)}, u32[]{:S(2)}, u32[]{:S(2)}) collective-permute-start(bf16[512,512]{0,1:T(8,128)(2,1)S(1)} %collective-permute-done.4), channel_id=1, source_target_pairs={{8,0},{16,8},{24,16},{32,24},{40,32},{48,40},{56,48},{64,56},{72,6... | collective-permute-start | bytes 1572872 | tf_op jit(solution)/shard_map/ppermute | solution.py:15
  52.5 110.0 %collective-permute-start.6 = (bf16[512,512]{0,1:T(8,128)(2,1)}, bf16[512,512]{0,1:T(8,128)(2,1)}, u32[]{:S(2)}, u32[]{:S(2)}) collective-permute-start(bf16[512,512]{0,1:T(8,128)(2,1)} %collective-permute-done.5), channel_id=1, source_target_pairs={{8,0},{16,8},{24,16},{32,24},{40,32},{48,40},{56,48},{64,56},{72,6... | collective-permute-start | bytes 1572872 | tf_op jit(solution)/shard_map/ppermute | solution.py:15
  82.3 10.6 %copy-start.7 = (bf16[512,512]{1,0:T(8,128)(2,1)S(1)}, bf16[512,512]{1,0:T(8,128)(2,1)}, u32[]{:S(2)}) copy-start(bf16[512,512]{1,0:T(8,128)(2,1)} %param.8) | copy-start | bytes 1572868
  82.3 11.6 %copy-start.8 = (bf16[512,512]{1,0:T(8,128)(2,1)S(1)}, bf16[512,512]{1,0:T(8,128)(2,1)}, u32[]{:S(2)}) copy-start(bf16[512,512]{1,0:T(8,128)(2,1)} %param.9) | copy-start | bytes 1572868
  162.5 72.1 %collective-permute-start.7 = (bf16[512,512]{0,1:T(8,128)(2,1)}, bf16[512,512]{0,1:T(8,128)(2,1)}, u32[]{:S(2)}, u32[]{:S(2)}) collective-permute-start(bf16[512,512]{0,1:T(8,128)(2,1)} %collective-permute-done.6), channel_id=1, source_target_pairs={{8,0},{16,8},{24,16},{32,24},{40,32},{48,40},{56,48},{64,56},{72,6... | collective-permute-start | bytes 1572872 | tf_op jit(solution)/shard_map/ppermute | solution.py:15
  228.7 7.9 %copy-start.2 = (bf16[512,2560]{1,0:T(8,128)(2,1)S(1)}, bf16[512,2560]{1,0:T(8,128)(2,1)}, u32[]{:S(2)}) copy-start(bf16[512,2560]{1,0:T(8,128)(2,1)} %select_n.44) | copy-start | bytes 7864324
  228.7 7.9 %copy-start.12 = (bf16[512,512]{0,1:T(8,128)(2,1)S(1)}, bf16[512,512]{0,1:T(8,128)(2,1)}, u32[]{:S(2)}) copy-start(bf16[512,512]{0,1:T(8,128)(2,1)} %copy.41) | copy-start | bytes 1572868
  228.7 7.9 %copy-start.13 = (bf16[512,512]{0,1:T(8,128)(2,1)S(1)}, bf16[512,512]{0,1:T(8,128)(2,1)}, u32[]{:S(2)}) copy-start(bf16[512,512]{0,1:T(8,128)(2,1)} %copy.42) | copy-start | bytes 1572868
  228.7 7.9 %copy-start.20 = (f32[512]{0:T(512)S(1)}, f32[512]{0:T(512)}, u32[]{:S(2)}) copy-start(f32[512]{0:T(512)} %param.12) | copy-start | bytes 6148
  241.0 0.8 copy-start.10
  241.8 16.5 %collective-permute-start = (bf16[512,512]{0,1:T(8,128)(2,1)S(1)}, bf16[512,512]{0,1:T(8,128)(2,1)S(1)}, u32[]{:S(2)}, u32[]{:S(2)}) collective-permute-start(bf16[512,512]{0,1:T(8,128)(2,1)S(1)} %get-tuple-element.31), channel_id=1, source_target_pairs={{0,8},{8,16},{16,24},{24,32},{32,40},{40,48},{48,56},{56,64},{64,7... | collective-permute-start | bytes 1572872 | tf_op jit(solution)/shard_map/ppermute | solution.py:15
  258.3 0.8 copy-start.14
  259.1 15.6 %collective-permute-start.1 = (bf16[512,512]{0,1:T(8,128)(2,1)S(1)}, bf16[512,512]{0,1:T(8,128)(2,1)S(1)}, u32[]{:S(2)}, u32[]{:S(2)}) collective-permute-start(bf16[512,512]{0,1:T(8,128)(2,1)S(1)} %collective-permute-done), channel_id=1, source_target_pairs={{0,8},{8,16},{16,24},{24,32},{32,40},{40,48},{48,56},{56,64},{64,7... | collective-permute-start | bytes 1572872 | tf_op jit(solution)/shard_map/ppermute | solution.py:15
  274.7 0.8 copy-start.16
  275.5 14.9 %collective-permute-start.2 = (bf16[512,512]{0,1:T(8,128)(2,1)S(1)}, bf16[512,512]{0,1:T(8,128)(2,1)}, u32[]{:S(2)}, u32[]{:S(2)}) collective-permute-start(bf16[512,512]{0,1:T(8,128)(2,1)S(1)} %collective-permute-done.1), channel_id=1, source_target_pairs={{0,8},{8,16},{16,24},{24,32},{32,40},{40,48},{48,56},{56,64},{64,7... | collective-permute-start | bytes 1572872 | tf_op jit(solution)/shard_map/ppermute | solution.py:15
  290.4 14.2 %collective-permute-start.3 = (bf16[512,512]{0,1:T(8,128)(2,1)}, bf16[512,512]{0,1:T(8,128)(2,1)}, u32[]{:S(2)}, u32[]{:S(2)}) collective-permute-start(bf16[512,512]{0,1:T(8,128)(2,1)} %collective-permute-done.2), channel_id=1, source_target_pairs={{0,8},{8,16},{16,24},{24,32},{32,40},{40,48},{48,56},{56,64},{64,7... | collective-permute-start | bytes 1572872 | tf_op jit(solution)/shard_map/ppermute | solution.py:15
  296.4 10.4 %copy-start.17 = (bf16[512,512]{0,1:T(8,128)(2,1)S(1)}, bf16[512,512]{0,1:T(8,128)(2,1)}, u32[]{:S(2)}) copy-start(bf16[512,512]{0,1:T(8,128)(2,1)} %copy-done.16) | copy-start | bytes 1572868
  296.4 10.4 %copy-start.15 = (bf16[512,512]{0,1:T(8,128)(2,1)S(1)}, bf16[512,512]{0,1:T(8,128)(2,1)}, u32[]{:S(2)}) copy-start(bf16[512,512]{0,1:T(8,128)(2,1)} %copy-done.14) | copy-start | bytes 1572868
  298.6 8.3 %copy-start.11 = (bf16[512,512]{0,1:T(8,128)(2,1)S(1)}, bf16[512,512]{0,1:T(8,128)(2,1)}, u32[]{:S(2)}) copy-start(bf16[512,512]{0,1:T(8,128)(2,1)} %copy-done.10) | copy-start | bytes 1572868
  307.0 1.5 copy-start.1
  393.5 5.4 copy-start.4
  393.5 5.4 copy-start.6
  397.9 1.0 copy-start
Sparse Core Ops, SparseCore 0:
  399.0 258.5 all-reduce.4
